TPU v7x, 256 devices: a whole 4x4x8 slice. The times are simulated.
256 devices in a mesh: req: 8 (over z), exp: 8 (over y, core), hid: 4 (over x).
Axes of the slice: x: 4, y: 4, z: 8, core: 2. Of those that a mesh axis runs over, the one named last changes fastest.
Arguments:
- layer_input_rows: bfloat16 [16384, 1536], P(('req', 'exp')), may hold values from -6 to 6
- attention_norm_gain: float32 [1536], replicated
- query_weight: bfloat16 [1536, 1536], P(None, 'hid'), may hold values from -1 to 1
- key_weight: bfloat16 [1536, 512], P(None, 'hid'), may hold values from -1 to 1
- value_weight: bfloat16 [1536, 512], P(None, 'hid'), may hold values from -0.15625 to 0.15625
- attention_output_weight: bfloat16 [1536, 1536], P('hid'), may hold values from -0.15625 to 0.15625
- query_down_factor: bfloat16 [64, 1536, 16], P(('req', 'exp')), may hold values from -0.15625 to 0.15625
- query_up_factor: bfloat16 [64, 16, 1536], P(('req', 'exp')), may hold values from -1.5 to 1.5
- value_down_factor: bfloat16 [64, 1536, 16], P(('req', 'exp')), may hold values from -0.15625 to 0.15625
- value_up_factor: bfloat16 [64, 16, 512], P(('req', 'exp')), may hold values from -1.5 to 1.5
- lengths: int32 [8, 4], P('req'), may hold values from 1 to 1024, 2048 in all within a row
- request_adapter: int32 [8, 4], replicated, may hold values from 0 to 63
- adapter_home_row: int32 [64], replicated, may hold values from 0 to 63, each once
- expert_norm_gain: float32 [1536], replicated, may hold values from 0.4 to 1.6
- routes: int32 [16384, 8], P(('req', 'exp', 'hid')), may hold values from 0 to 39, all different within a row; in each aligned block of 64 rows (0 to 63, 64 to 127, ...) at most 16 rows name the same one
- router_expert_weight: float32 [16384, 8], P(('req', 'exp', 'hid')), may hold values from 0.1 to 0.5
- expert_gate_weight: bfloat16 [40, 1536, 512], P('exp', None, 'hid'), may hold values from -0.15625 to 0.15625
- expert_up_weight: bfloat16 [40, 1536, 512], P('exp', None, 'hid'), may hold values from -0.15625 to 0.15625
- expert_down_weight: bfloat16 [40, 512, 1536], P('exp', 'hid'), may hold values from -0.25 to 0.25
Outputs:
- attn_out: bfloat16 [16384, 1536], P(('req', 'exp', 'hid'))
- expert_out: bfloat16 [16384, 1536], P(('req', 'exp', 'hid'))
Inputs may be any that keep to these rules, and one draw needn't show every extreme that they name: `lengths`: each row sums to 2048; its largest entry is exactly 1024. `adapter_home_row`: each adapter row appears once. `routes`: A row names 8 different experts. In the rows of one device (64 consecutive rows, aligned) no expert is named more than 16 times, a bound that some block reaches in some of them.
All inputs are finite; a program needn't handle non-finite values.
Results may differ from a plain program's by a relative error of at most 0.029.
The roundings to bfloat16 on the way count: a program that leaves them out, or rounds other values in their place, can miss the bound.
Values may be sent and summed in bfloat16 or wider, within the bound.
No kernel may reach another device: no remote copies, remote signals or barrier semaphores. Data moves between devices by JAX's collectives and lax.ppermute only.
A program may use at most 128 MiB of HBM per device.

v0:
```python
import jax
import jax.numpy as jnp
from jax import lax
from jax.sharding import PartitionSpec as P

HEAD_WIDTH = 64
scale_attn = 0.015625
residual_mult = 0.22
norm_eps = 1e-06
rope_base = 10000.0
neg_large = -1e30


def rms_norm(values, norm_gain):
    widened = values.astype(jnp.float32)
    mean_sq = jnp.mean(widened * widened, axis=-1, keepdims=True)
    return (widened * lax.rsqrt(mean_sq + norm_eps) * norm_gain).astype(jnp.bfloat16)


def rotary(heads_in, position):
    half_size = heads_in.shape[-1] // 2
    frequency = rope_base ** (-2.0 * jnp.arange(half_size, dtype=jnp.float32) / heads_in.shape[-1])
    angles = position.astype(jnp.float32)[:, None] * frequency[None, :]
    cosine = jnp.cos(angles)[:, None, :]
    sine_part = jnp.sin(angles)[:, None, :]
    first_half = heads_in[..., :half_size]
    second_half = heads_in[..., half_size:]
    return jnp.concatenate(
        [
            first_half * cosine - second_half * sine_part,
            second_half * cosine + first_half * sine_part,
        ],
        axis=-1,
    )


def request_of(row_ids, group_len):
    request_end = jnp.cumsum(group_len)
    return jnp.sum((row_ids[:, None] >= request_end[None, :]).astype(jnp.int32), axis=1)


def locate(row_ids, group_len):
    request_end = jnp.cumsum(group_len)
    request_start = request_end - group_len
    request = request_of(row_ids, group_len)
    member = request[:, None] == jnp.arange(group_len.shape[0], dtype=jnp.int32)[None, :]
    position = row_ids - jnp.sum(jnp.where(member, request_start[None, :], 0), axis=1)
    return (request, member, position)


def expert_rows(rows_in, expert_gate_weight, expert_up_weight, expert_down_weight):
    gate_act = jnp.einsum(
        "red,edf->ref", rows_in, expert_gate_weight, preferred_element_type=jnp.float32
    )
    upper = jnp.einsum(
        "red,edf->ref", rows_in, expert_up_weight, preferred_element_type=jnp.float32
    )
    hidden = (jax.nn.silu(gate_act) * upper).astype(jnp.bfloat16)
    return jnp.einsum(
        "ref,efd->red", hidden, expert_down_weight, preferred_element_type=jnp.float32
    )


def per_device(
    layer_input_rows,
    attention_norm_gain,
    query_weight,
    key_weight,
    value_weight,
    attention_output_weight,
    query_down_factor,
    query_up_factor,
    value_down_factor,
    value_up_factor,
    lengths,
    request_adapter,
    adapter_home_row,
    expert_norm_gain,
    routes,
    router_expert_weight,
    expert_gate_weight,
    expert_up_weight,
    expert_down_weight,
):
    exp_count = lax.axis_size("exp")
    hid_count = lax.axis_size("hid")
    exp_index = lax.axis_index("exp")
    hid_index = lax.axis_index("hid")
    req_index = lax.axis_index("req")
    query_rows = layer_input_rows.shape[0]
    width = layer_input_rows.shape[1]
    kv_local = key_weight.shape[1] // HEAD_WIDTH
    q_local = query_weight.shape[1] // HEAD_WIDTH
    group_share = q_local // kv_local
    adapter_rank_size = query_down_factor.shape[2]
    requests = lengths.shape[1]
    group_len = lengths[0]
    row_ids = exp_index * query_rows + jnp.arange(query_rows, dtype=jnp.int32)
    request, member, position = locate(row_ids, group_len)
    wanted = lax.dynamic_index_in_dim(request_adapter, req_index, 0, keepdims=False)
    slot_ids = jnp.arange(adapter_home_row.shape[0], dtype=jnp.int32)
    home_of = jnp.sum(
        jnp.where(wanted[:, None] == slot_ids[None, :], adapter_home_row[None, :], 0), axis=1
    )
    query_cols = q_local * HEAD_WIDTH
    kv_cols = kv_local * HEAD_WIDTH
    bank_local = query_down_factor.shape[0]
    up_q = lax.dynamic_slice_in_dim(query_up_factor, hid_index * query_cols, query_cols, 2)
    up_v = lax.dynamic_slice_in_dim(value_up_factor, hid_index * kv_cols, kv_cols, 2)
    parts_in = (query_down_factor, up_q, value_down_factor, up_v)
    part_shapes = [p.shape[1:] for p in parts_in]
    part_sizes = [p.shape[1] * p.shape[2] for p in parts_in]
    bank = jnp.concatenate([p.reshape(bank_local, -1) for p in parts_in], axis=1)
    along_req = lax.all_gather(bank, "req", axis=0, tiled=True)
    home_dev = home_of // bank_local
    home_pick = home_dev // exp_count * bank_local + home_of % bank_local
    mine = home_dev % exp_count == exp_index
    rows_pick = jnp.take(along_req, home_pick, axis=0)
    rows_pick = jnp.where(mine[:, None], rows_pick, jnp.zeros_like(rows_pick))
    rows_pick = lax.psum(rows_pick, "exp")
    chosen = []
    start = 0
    for shape_in, size_in in zip(part_shapes, part_sizes):
        chosen.append(rows_pick[:, start : start + size_in].reshape((requests,) + shape_in))
        start += size_in
    qa_sel, qb_sel, va_sel, vb_sel = chosen
    normed_rows = rms_norm(layer_input_rows, attention_norm_gain)

    def low_rank_term(a_sel, b_sel, width_cols, offset):
        inner_terms = jnp.einsum(
            "td,jdr->tjr", normed_rows, a_sel, preferred_element_type=jnp.float32
        )
        inner_terms = (
            jnp.where(member[:, :, None], inner_terms, 0.0)
            .reshape(query_rows, requests * adapter_rank_size)
            .astype(jnp.bfloat16)
        )
        right_factor = b_sel.reshape(requests * adapter_rank_size, width_cols)
        return jnp.dot(inner_terms, right_factor, preferred_element_type=jnp.float32)

    query_matrix = jnp.dot(
        normed_rows, query_weight, preferred_element_type=jnp.float32
    ) + low_rank_term(qa_sel, qb_sel, query_cols, hid_index * query_cols)
    query_matrix = rotary(query_matrix.reshape(query_rows, q_local, HEAD_WIDTH), position).astype(
        jnp.bfloat16
    )
    query_matrix = query_matrix.reshape(query_rows, kv_local, group_share, HEAD_WIDTH)
    keys_own = jnp.dot(normed_rows, key_weight, preferred_element_type=jnp.float32)
    keys_own = (
        rotary(keys_own.reshape(query_rows, kv_local, HEAD_WIDTH), position)
        .astype(jnp.bfloat16)
        .reshape(query_rows, kv_cols)
    )
    values_own = jnp.dot(
        normed_rows, value_weight, preferred_element_type=jnp.float32
    ) + low_rank_term(va_sel, vb_sel, kv_cols, hid_index * kv_cols)
    values_own = values_own.astype(jnp.bfloat16)
    running_max = jnp.full((kv_local, group_share, query_rows), neg_large, jnp.float32)
    key_piece = lax.all_gather(keys_own, "exp", axis=0, tiled=True)
    value_piece = lax.all_gather(values_own, "exp", axis=0, tiled=True)
    piece_len = key_piece.shape[0]
    key_ids = jnp.arange(piece_len, dtype=jnp.int32)
    key_request = request_of(key_ids, group_len)
    allowed = (request[:, None] == key_request[None, :]) & (key_ids[None, :] <= row_ids[:, None])
    key_heads = key_piece.reshape(piece_len, kv_local, HEAD_WIDTH)
    value_heads = value_piece.reshape(piece_len, kv_local, HEAD_WIDTH)
    scores = (
        jnp.einsum("qkgh,nkh->kgqn", query_matrix, key_heads, preferred_element_type=jnp.float32)
        * scale_attn
    )
    scores = jnp.where(allowed[None, None], scores, neg_large)
    new_max = jnp.maximum(running_max, jnp.max(scores, axis=-1))
    weights = jnp.where(allowed[None, None], jnp.exp(scores - new_max[..., None]), 0.0)
    running_sum = jnp.sum(weights, axis=-1)
    running_out = jnp.einsum(
        "kgqn,nkh->kgqh",
        weights.astype(jnp.bfloat16),
        value_heads,
        preferred_element_type=jnp.float32,
    )
    running_max, running_sum, running_out = (new_max, running_sum, running_out)
    attended = (running_out / running_sum[..., None]).astype(jnp.bfloat16)
    attended = jnp.transpose(attended, (2, 0, 1, 3)).reshape(query_rows, query_cols)
    tok_rows = query_rows // hid_count
    attn_out = lax.psum_scatter(
        jnp.dot(attended, attention_output_weight, preferred_element_type=jnp.float32).astype(
            jnp.bfloat16
        ),
        "hid",
        scatter_dimension=0,
        tiled=True,
    )
    own_rows = lax.dynamic_slice_in_dim(layer_input_rows, hid_index * tok_rows, tok_rows, 0)
    mixed_rows = own_rows.astype(jnp.float32) + residual_mult * attn_out.astype(jnp.float32)
    normed_moe = rms_norm(mixed_rows, expert_norm_gain)
    local_exp = expert_gate_weight.shape[0]
    expert_count = local_exp * exp_count
    top_count = routes.shape[1]
    capacity = max(2, tok_rows // 4)
    flat_route = routes.reshape(tok_rows * top_count)
    route_hits = (flat_route[:, None] == jnp.arange(expert_count, dtype=jnp.int32)[None, :]).astype(
        jnp.int32
    )
    earlier = jnp.cumsum(route_hits, axis=0) - route_hits
    slot_pos = jnp.sum(earlier * route_hits, axis=1)
    slots = slot_pos * expert_count + flat_route
    slot_table = jnp.arange(capacity * expert_count, dtype=jnp.int32)
    placed = jnp.any(
        slot_table[:, None, None] == slots.reshape(tok_rows, top_count)[None], axis=2
    ).astype(jnp.bfloat16)
    outgoing = jnp.dot(placed, normed_moe, preferred_element_type=jnp.float32).astype(jnp.bfloat16)
    outgoing = outgoing.reshape(capacity, expert_count, width)
    copies = jnp.broadcast_to(
        outgoing.reshape(capacity, exp_count, 1, local_exp, width),
        (capacity, exp_count, hid_count, local_exp, width),
    )
    copies = copies.reshape(capacity, exp_count * hid_count * local_exp, width)
    arrived = lax.all_to_all(copies, ("exp", "hid"), split_axis=1, concat_axis=0, tiled=True)
    partials = expert_rows(
        arrived, expert_gate_weight, expert_up_weight, expert_down_weight
    ).astype(jnp.bfloat16)
    returned = lax.all_to_all(partials, ("exp", "hid"), split_axis=0, concat_axis=1, tiled=True)
    returned = returned.reshape(capacity, exp_count, hid_count, local_exp, width)
    results = jnp.sum(returned.astype(jnp.float32), axis=2).astype(jnp.bfloat16)
    results = results.reshape(capacity * expert_count, width)
    picked = jnp.take(results, slots, axis=0).reshape(tok_rows, top_count, width)
    expert_out = jnp.sum(
        router_expert_weight[:, :, None] * picked.astype(jnp.float32), axis=1
    ).astype(jnp.bfloat16)
    return (attn_out, expert_out)


def solution(mesh):
    in_specs = (
        P(("req", "exp"), None),
        P(),
        P(None, "hid"),
        P(None, "hid"),
        P(None, "hid"),
        P("hid", None),
        P(("req", "exp"), None, None),
        P(("req", "exp"), None, None),
        P(("req", "exp"), None, None),
        P(("req", "exp"), None, None),
        P("req", None),
        P(),
        P(),
        P(),
        P(("req", "exp", "hid"), None),
        P(("req", "exp", "hid"), None),
        P("exp", None, "hid"),
        P("exp", None, "hid"),
        P("exp", "hid", None),
    )
    out_specs = (P(("req", "exp", "hid"), None), P(("req", "exp", "hid"), None))
    return jax.shard_map(
        per_device, mesh=mesh, in_specs=in_specs, out_specs=out_specs, check_vma=False
    )
```

profile of v0, /device:TPU:1, one launch (start us, length us, event | category | flops | bytes accessed | tf_op | source)
XLA Modules:
  0.0 535.5 jit_solution(14082683978876960325)
XLA Ops:
  7.2 0.8 dynamic-slice_bitcast_fusion
  8.1 0.7 dynamic-slice_bitcast_fusion.1
  8.8 1.0 copy.99
  10.1 1.0 copy.100
  11.7 29.4 %all-gather = bf16[8,1,57344]{2,1,0:T(2,128)(2,1)S(1)} all-gather(bf16[1,1,57344]{2,1,0:T(2,128)(2,1)S(1)} %maximum_bitcast_fusion), channel_id=1, replica_groups=mesh['req'=8,'exp'=8,'hid'=4] {'req'}, dimensions={0}, use_global_device_ids=true | all-gather | bytes 1032192 | tf_op jit(solution)/shard_map/all_gather | solution.py:114
  41.0 1.0 copy.131
  42.5 1.0 gather_fusion
  43.5 1.1 select_select_fusion
  44.7 1.4 fusion.7
  46.6 2.6 fusion.56
  49.8 1.2 fusion.6
  51.8 19.2 %all_gather.9 = bf16[2048,128]{0,1:T(8,128)(2,1)} all-gather(bf16[256,128]{0,1:T(8,128)(2,1)S(1)} %bitcast.160), channel_id=1, replica_groups=mesh['req'=8,'exp'=8,'hid'=4] {'exp'}, dimensions={0}, use_global_device_ids=true | all-gather | bytes 589824 | tf_op jit(solution)/shard_map/all_gather | solution.py:159
  71.1 41.2 %all-reduce.2.cloned.1.call-done = bf16[4,57344]{1,0:T(4,128)(2,1)} async-done(((bf16[4,57344]{1,0:T(4,128)(2,1)}), bf16[4,57344]{1,0:T(4,128)(2,1)}) %all-reduce.2.cloned.1.call-update) | async-done | bytes 458768 | tf_op jit(solution)/shard_map/psum | solution.py:120
  112.3 1.9 fusion.60
  114.2 2.1 reshape.381
  116.2 1.3 copy.101
  117.5 2.2 fusion.54
  119.7 2.1 reshape.383
  121.8 1.3 copy.103
  123.1 1.7 fusion.51
  124.8 0.8 slice.49
  125.7 0.9 select_convert_fusion.1
  127.1 7.7 %fusion = (f32[2,3,256]{2,1,0:T(4,128)S(1)}, f32[2,2048,256,3]{2,1,3,0:T(8,128)}) fusion(pred[256,2048]{0,1:T(8,128)(4,1)S(1)} %copy-done.2, bf16[2048,2,64,1]{0,2,3,1:T(8,128)(2,1)} %bitcast.158, bf16[256,2,3,32]{0,3,2,1:T(8,128)(2,1)S(1)} %bitcast.169, bf16[256,2,3,32]{0,3,2,1:T(8,128)(2,1)S(1)} %bitcast.168), kind=kOutput, calls=%fused_computation.4 | convolution fusion | flops 412482048 | bytes 13834240 | tf_op jit(solution)/shard_map/qkgh,nkh->kgqn/dot_general | solution.py:168
  135.0 1.4 fusion.21
  136.5 15.9 %all_gather.11 = bf16[2048,128]{1,0:T(8,128)(2,1)S(1)} all-gather(bf16[256,128]{1,0:T(8,128)(2,1)S(1)} %fusion.21), channel_id=1, replica_groups=mesh['req'=8,'exp'=8,'hid'=4] {'exp'}, dimensions={0}, use_global_device_ids=true | all-gather | bytes 589824 | tf_op jit(solution)/shard_map/all_gather | solution.py:160
  152.6 6.9 %fusion.1 = f32[2,3,256]{2,1,0:T(4,128)S(1)} fusion(f32[2,2048,256,3]{2,1,3,0:T(8,128)} %get-tuple-element.17, f32[2,3,256]{2,1,0:T(4,128)S(1)} %broadcast_maximum_fusion, pred[256,2048]{0,1:T(8,128)(4,1)S(1)} %copy-done.2), kind=kLoop, calls=%fused_computation.5 | loop fusion | flops 15727104 | bytes 13119488 | tf_op jit(solution)/shard_map/reduce_sum | solution.py:174
  159.5 1.4 copy-done.1
  160.8 3.6 fusion.25
  164.5 1.5 convolution_convert_fusion.1
  166.3 1.2 reduce-window.11
  168.6 19.8 %reduce-scatter.2.cloned.1.call-done = bf16[64,1536]{1,0:T(8,128)(2,1)} async-done(((bf16[256,1536]{1,0:T(8,128)(2,1)}), bf16[64,1536]{1,0:T(8,128)(2,1)}) %reduce-scatter.2.cloned.1.call-update) | async-done | bytes 196624 | tf_op jit(solution)/shard_map/reduce_scatter | solution.py:185
  188.4 1.1 multiply_reduce_fusion.1
  189.5 3.0 convolution_convert_fusion
  192.5 4.3 broadcast_in_dim.153
  196.7 3.2 copy.113
  199.9 1.0 broadcast_in_dim.154
  200.9 98.1 %all_to_all.33 = bf16[16,160,1536]{2,0,1:T(8,128)(2,1)S(1)} all-to-all(bf16[16,160,1536]{2,0,1:T(8,128)(2,1)S(1)} %bitcast.152), channel_id=1, replica_groups=mesh['req'=8,'exp'=8,'hid'=4] {'exp','hid'}, dimensions={1} | all-to-all | bytes 15728640 | tf_op jit(solution)/shard_map/all_to_all | solution.py:218
  298.9 3.9 copy.114
  302.8 6.0 %convolution_bitcast_fusion.1 = f32[512,5,128]{2,0,1:T(8,128)S(1)} fusion(bf16[512,5,1536]{2,0,1:T(8,128)(2,1)} %bitcast.155, bf16[5,1536,128]{2,1,0:T(8,128)(2,1)} %param.35), kind=kOutput, calls=%fused_computation.23 | convolution fusion | flops 1006632960 | bytes 11141120 | tf_op jit(solution)/shard_map/red,edf->ref/dot_general | solution.py:52
  308.8 12.2 %convert_bitcast_fusion = bf16[512,5,1536]{2,0,1:T(8,128)(2,1)} fusion(bf16[5,128,1536]{2,1,0:T(8,128)(2,1)S(1)} %copy-done, bf16[512,5,1536]{2,0,1:T(8,128)(2,1)} %bitcast.156, bf16[5,1536,128]{2,1,0:T(8,128)(2,1)} %param.36, f32[512,5,128]{2,0,1:T(8,128)S(1)} %convolution_bitcast_fusion.1), kind=kOutput, calls=%fused_computation.7 | convolution fusion | flops 2019164160 | bytes 20971520 | tf_op jit(solution)/shard_map/ref,efd->red/dot_general | solution.py:59
  321.0 12.0 %copy.115 = bf16[512,5,1536]{2,1,0:T(8,128)(2,1)} copy(bf16[512,5,1536]{2,0,1:T(8,128)(2,1)} %convert_bitcast_fusion) | data formatting | bytes 15728640 | tf_op jit(solution)/shard_map/convert_element_type | solution.py:221
  332.9 5.2 all-to-all-start.1
  339.1 163.1 %all-to-all-done.1 = bf16[512,5,1536]{2,1,0:T(8,128)(2,1)} async-done(((bf16[512,5,1536]{2,1,0:T(8,128)(2,1)}), bf16[512,5,1536]{2,1,0:T(8,128)(2,1)}, u32[]{:S(2)}, u32[]{:S(2)}) %all-to-all-start.1) | async-done | bytes 7864352 | tf_op jit(solution)/shard_map/all_to_all | solution.py:222
  502.1 10.2 %reduce.1 = bf16[16,8,5,1536]{3,2,0,1:T(8,128)(2,1)} reduce(bf16[16,8,4,5,1536]{4,3,0,2,1:T(8,128)(2,1)} %bitcast.41, bf16[]{:T(256)} %constant.141.clone.1), dimensions={2}, to_apply=%region_15.16 | reduce | flops 2949120 | bytes 9830402 | tf_op jit(solution)/shard_map/reduce_sum | solution.py:224
  512.3 3.9 copy.117
  516.2 4.3 reshape.389
  520.5 5.4 %gather_fusion.1 = bf16[512,1536]{1,0:T(8,128)(2,1)S(1)} fusion(bf16[640,1536]{1,0:T(8,128)(2,1)} %reshape.389, s32[1024]{0:T(1024)S(1)} %pad_clamp_fusion), kind=kCustom, calls=%fused_computation.1 | custom fusion | bytes 3147776 | tf_op jit(solution)/shard_map/jit(_take)/gather | solution.py:226
  525.9 2.8 multiply_reduce_fusion
  (99 shorter events, 6.4 us)
Async XLA Ops:
  7.2 301.6 %copy-start = (bf16[5,128,1536]{2,1,0:T(8,128)(2,1)S(1)}, bf16[5,128,1536]{2,1,0:T(8,128)(2,1)}, u32[]{:S(2)}) copy-start(bf16[5,128,1536]{2,1,0:T(8,128)(2,1)} %param.37) | copy-start | bytes 5898244
  7.2 105.1 %all-reduce.2.cloned.1.call-start = ((), (), s32[]{:S(2)}) async-start(), calls=%async_computation.3 | async-start | bytes 917504 | tf_op jit(solution)/shard_map/psum | solution.py:120
  11.7 30.4 %copy-start.15 = (s32[8,4]{0,1:T(4,128)S(1)}, s32[8,4]{0,1:T(4,128)}, u32[]{:S(2)}) copy-start(s32[8,4]{0,1:T(4,128)} %param.30) | copy-start | bytes 388
  11.7 30.6 %copy-start.19 = (s32[64]{0:T(128)S(1)}, s32[64]{0:T(128)}, u32[]{:S(2)}) copy-start(s32[64]{0:T(128)} %param.31) | copy-start | bytes 772
  43.5 2.6 copy-start.20
  43.5 3.1 copy-start.3
  43.5 3.1 copy-start.17
  44.6 4.6 copy-start.16
  44.6 143.7 %reduce-scatter.2.cloned.1.call-start = ((), (), s32[]{:S(2)}) async-start(), calls=%async_computation.4 | async-start | bytes 983040 | tf_op jit(solution)/shard_map/reduce_scatter | solution.py:185
  51.2 0.6 copy-start.8
  51.2 0.6 copy-start.10
  123.1 3.4 copy-start.7
  123.1 3.9 copy-start.9
  123.1 3.9 copy-start.11
  123.1 3.9 copy-start.2
  127.0 7.8 %slice-start = ((bf16[4,57344]{1,0:T(4,128)(2,1)}), bf16[4,2048]{1,0:T(4,128)(2,1)S(1)}, s32[]{:S(2)}) async-start(bf16[4,57344]{1,0:T(4,128)(2,1)} %all-reduce.2.cloned.1.call-done), calls=%async_computation.5 | async-start | bytes 32768 | tf_op jit(solution)/shard_map/slice | solution.py:124
  127.1 8.0 %copy-start.4 = (bf16[256,1536]{1,0:T(8,128)(2,1)S(1)}, bf16[256,1536]{1,0:T(8,128)(2,1)}, u32[]{:S(2)}) copy-start(bf16[256,1536]{1,0:T(8,128)(2,1)} %param.19) | copy-start | bytes 2359300
  127.1 8.0 %copy-start.18 = (f32[1536]{0:T(1024)S(1)}, f32[1536]{0:T(1024)}, u32[]{:S(2)}) copy-start(f32[1536]{0:T(1024)} %param.20) | copy-start | bytes 18436
  152.6 8.2 %copy-start.1 = (f32[2,2048,256,3]{2,1,3,0:T(8,128)S(1)}, f32[2,2048,256,3]{2,1,3,0:T(8,128)}, u32[]{:S(2)}) copy-start(f32[2,2048,256,3]{2,1,3,0:T(8,128)} %get-tuple-element.17) | copy-start | bytes 37748740
  160.8 3.6 copy-start.6
  164.5 1.5 copy-start.12
  164.5 23.9 %copy-start.5 = (bf16[256,1536]{1,0:T(8,128)(2,1)S(1)}, bf16[256,1536]{1,0:T(8,128)(2,1)}, u32[]{:S(2)}) copy-start(bf16[256,1536]{1,0:T(8,128)(2,1)} %param.19) | copy-start | bytes 2359300
  164.5 25.0 %copy-start.13 = (f32[1536]{0:T(1024)S(1)}, f32[1536]{0:T(1024)}, u32[]{:S(2)}) copy-start(f32[1536]{0:T(1024)} %param.32) | copy-start | bytes 18436
  332.9 5.4 %copy-start.14 = (f32[64,8]{0,1:T(8,128)S(1)}, f32[64,8]{0,1:T(8,128)}, u32[]{:S(2)}) copy-start(f32[64,8]{0,1:T(8,128)} %param.34) | copy-start | bytes 6148
  332.9 169.2 %all-to-all-start.1 = ((bf16[512,5,1536]{2,1,0:T(8,128)(2,1)}), bf16[512,5,1536]{2,1,0:T(8,128)(2,1)}, u32[]{:S(2)}, u32[]{:S(2)}) async-start(bf16[512,5,1536]{2,1,0:T(8,128)(2,1)} %copy.115), calls=%async_computation.2 | async-start | bytes 25165824 | tf_op jit(solution)/shard_map/all_to_all | solution.py:222
Sparse Core Ops, SparseCore 0:
  44.7 67.4 all-reduce.1
  166.1 22.1 reduce-scatter.1
where the time goes:
time: 537 us; the launch traced here: 536 us
  waiting for transfers between devices  224 us (42%)
  blocking collectives  163 us (30%)
  local copies, waits for them, and re-layouts  57.7 us (11%)
  matrix products  42.8 us (8%)
  other arithmetic  28.6 us (5%)
  between operations  14.6 us (3%)
    all_to_all x1, waiting for transfers between devices, per_device(): lax.all_to_all(partials, ('exp', 'hid'), split_axis=0, concat_axis=1, til...  163 us
    all_to_all x1, blocking collectives, per_device(): lax.all_to_all(copies, ('exp', 'hid'), split_axis=1, concat_axis=0, tiled...  98.1 us
    psum x1, waiting for transfers between devices, per_device(): rows_pick = lax.psum(rows_pick, 'exp')  41.2 us
    all_gather x1, blocking collectives, per_device(): along_req = lax.all_gather(bank, 'req', axis=0, tiled=True)  29.4 us
    reduce_scatter x1, waiting for transfers between devices, per_device(): lax.psum_scatter(jnp.dot(attended, attention_output_weight, preferred_ele...  19.8 us
    all_gather x1, blocking collectives, per_device(): key_piece = lax.all_gather(keys_own, 'exp', axis=0, tiled=True)  19.2 us
    all_gather x1, blocking collectives, per_device(): value_piece = lax.all_gather(values_own, 'exp', axis=0, tiled=True)  15.9 us
    dot_general x1, matrix products, expert_rows(): jnp.einsum('ref,efd->red', hidden, expert_down_weight, preferred_element_...  12.2 us
  transfers between devices with their start and end apart: 3, of which 3 were waited for; matrix products, arithmetic and copies ran while one was open for 2% of the time, Pallas kernels for 0%

commit v1 on v0

--- a/solution.py
+++ b/solution.py
@@ -82,6 +82,18 @@
     expert_up_weight,
     expert_down_weight,
 ):
+
+    def vectors_wait(array_in):
+        return jnp.concatenate(
+            lax.all_to_all(
+                jnp.stack(jnp.split(array_in, lax.axis_size(("exp", "hid")), 0), axis=0),
+                ("exp", "hid"),
+                0,
+                0,
+            ),
+            1,
+        )
+
     exp_count = lax.axis_size("exp")
     hid_count = lax.axis_size("hid")
     exp_index = lax.axis_index("exp")
@@ -219,7 +231,7 @@
     partials = expert_rows(
         arrived, expert_gate_weight, expert_up_weight, expert_down_weight
     ).astype(jnp.bfloat16)
-    returned = lax.all_to_all(partials, ("exp", "hid"), split_axis=0, concat_axis=1, tiled=True)
+    returned = vectors_wait(partials)
     returned = returned.reshape(capacity, exp_count, hid_count, local_exp, width)
     results = jnp.sum(returned.astype(jnp.float32), axis=2).astype(jnp.bfloat16)
     results = results.reshape(capacity * expert_count, width)

time: 537 us -> 506 us (0.942)
  waiting for transfers between devices: 224 us -> 151 us
  local copies, waits for them, and re-layouts: 57.7 us -> 98.6 us
    all_to_all x1, waiting for transfers between devices: 163 us -> 91.3 us  [vectors_wait(): lax.all_to_all(jnp.stack(jnp.split(array_in, lax.axis_size(('exp', 'hid')...]
    unnamed x51 -> x68, local copies, waits for them, and re-layouts: 7.44 us -> 58.3 us
    convert_element_type x1 -> x0, local copies, waits for them, and re-layouts: 12 us -> none  [per_device(): partials = expert_rows(arrived, expert_gate_weight, expert_up_weight, exp...]
where the time goes in v1:
time: 506 us; the launch traced here: 502 us
  blocking collectives  162 us (32%)
  waiting for transfers between devices  151 us (30%)
  local copies, waits for them, and re-layouts  98.6 us (19%)
  matrix products  45.4 us (9%)
  other arithmetic  25.3 us (5%)
  between operations  14.5 us (3%)
  starting transfers between devices  5.2 us (1%)
    all_to_all x1, blocking collectives, per_device(): lax.all_to_all(copies, ('exp', 'hid'), split_axis=1, concat_axis=0, tiled...  98.1 us
    all_to_all x1, waiting for transfers between devices, vectors_wait(): lax.all_to_all(jnp.stack(jnp.split(array_in, lax.axis_size(('exp', 'hid')...  91.3 us
    unnamed x68, local copies, waits for them, and re-layouts  58.3 us
    psum x1, waiting for transfers between devices, per_device(): rows_pick = lax.psum(rows_pick, 'exp')  39.7 us
    all_gather x1, blocking collectives, per_device(): along_req = lax.all_gather(bank, 'req', axis=0, tiled=True)  29.4 us
    reduce_scatter x1, waiting for transfers between devices, per_device(): lax.psum_scatter(jnp.dot(attended, attention_output_weight, preferred_ele...  19.8 us
    all_gather x1, blocking collectives, per_device(): key_piece = lax.all_gather(keys_own, 'exp', axis=0, tiled=True)  19.1 us
    all_gather x1, blocking collectives, per_device(): value_piece = lax.all_gather(values_own, 'exp', axis=0, tiled=True)  15.9 us
  transfers between devices with their start and end apart: 3, of which 3 were waited for; matrix products, arithmetic and copies ran while one was open for 2% of the time, Pallas kernels for 0%

profile of v1, /device:TPU:1, one launch (start us, length us, event | category | flops | bytes accessed | tf_op | source)
XLA Modules:
  0.0 502.1 jit_solution(15372367332503674267)
XLA Ops:
  11.7 29.4 %all-gather = bf16[8,1,57344]{2,1,0:T(2,128)(2,1)S(1)} all-gather(bf16[1,1,57344]{2,1,0:T(2,128)(2,1)S(1)} %maximum_bitcast_fusion), channel_id=1, replica_groups=mesh['req'=8,'exp'=8,'hid'=4] {'req'}, dimensions={0}, use_global_device_ids=true | all-gather | bytes 1032192 | tf_op jit(solution)/shard_map/all_gather | solution.py:126
  47.8 2.9 fusion.88
  50.7 1.7 fusion.90
  54.6 19.1 %all_gather.9 = bf16[2048,128]{0,1:T(8,128)(2,1)} all-gather(bf16[256,128]{0,1:T(8,128)(2,1)S(1)} %bitcast.284), channel_id=1, replica_groups=mesh['req'=8,'exp'=8,'hid'=4] {'exp'}, dimensions={0}, use_global_device_ids=true | all-gather | bytes 589824 | tf_op jit(solution)/shard_map/all_gather | solution.py:171
  73.7 39.7 %all-reduce.2.cloned.1.call-done = bf16[4,57344]{1,0:T(4,128)(2,1)} async-done(((bf16[4,57344]{1,0:T(4,128)(2,1)}), bf16[4,57344]{1,0:T(4,128)(2,1)}) %all-reduce.2.cloned.1.call-update) | async-done | bytes 458768 | tf_op jit(solution)/shard_map/psum | solution.py:132
  113.3 1.9 fusion.92
  115.2 2.1 reshape.380
  118.6 2.2 fusion.86
  120.8 2.1 reshape.382
  129.8 7.9 %fusion = (f32[2,3,256]{2,1,0:T(4,128)S(1)}, f32[2,2048,256,3]{2,1,3,0:T(8,128)}) fusion(pred[256,2048]{0,1:T(8,128)(4,1)} %fusion.6, bf16[2048,2,64,1]{0,2,3,1:T(8,128)(2,1)} %bitcast.282, bf16[256,2,3,32]{0,3,2,1:T(8,128)(2,1)S(1)} %bitcast.293, bf16[256,2,3,32]{0,3,2,1:T(8,128)(2,1)S(1)} %bitcast.292), kind=kOutput, calls=%fused_computation.4 | convolution fusion | flops 412482048 | bytes 13834240 | tf_op jit(solution)/shard_map/qkgh,nkh->kgqn/dot_general | solution.py:180
  139.3 15.9 %all_gather.11 = bf16[2048,128]{1,0:T(8,128)(2,1)S(1)} all-gather(bf16[256,128]{1,0:T(8,128)(2,1)S(1)} %fusion.21), channel_id=1, replica_groups=mesh['req'=8,'exp'=8,'hid'=4] {'exp'}, dimensions={0}, use_global_device_ids=true | all-gather | bytes 589824 | tf_op jit(solution)/shard_map/all_gather | solution.py:172
  156.3 7.5 %fusion.1 = f32[2,3,256]{2,1,0:T(4,128)S(1)} fusion(f32[2,2048,256,3]{2,1,3,0:T(8,128)} %get-tuple-element.17, f32[2,3,256]{2,1,0:T(4,128)S(1)} %broadcast_maximum_fusion, pred[256,2048]{0,1:T(8,128)(4,1)S(1)} %copy-done.2), kind=kLoop, calls=%fused_computation.5 | loop fusion | flops 15727104 | bytes 13119488 | tf_op jit(solution)/shard_map/reduce_sum | solution.py:186
  164.6 3.6 fusion.25
  172.3 19.8 %reduce-scatter.2.cloned.1.call-done = bf16[64,1536]{1,0:T(8,128)(2,1)} async-done(((bf16[256,1536]{1,0:T(8,128)(2,1)}), bf16[64,1536]{1,0:T(8,128)(2,1)}) %reduce-scatter.2.cloned.1.call-update) | async-done | bytes 196624 | tf_op jit(solution)/shard_map/reduce_scatter | solution.py:197
  193.2 3.0 convolution_convert_fusion
  196.2 4.3 broadcast_in_dim.153
  200.5 3.2 copy.107
  204.6 98.1 %all_to_all.23 = bf16[16,160,1536]{2,0,1:T(8,128)(2,1)S(1)} all-to-all(bf16[16,160,1536]{2,0,1:T(8,128)(2,1)S(1)} %bitcast.276), channel_id=1, replica_groups=mesh['req'=8,'exp'=8,'hid'=4] {'exp','hid'}, dimensions={1} | all-to-all | bytes 15728640 | tf_op jit(solution)/shard_map/all_to_all | solution.py:230
  302.7 3.9 copy.108
  306.5 6.0 %convolution_bitcast_fusion.1 = f32[512,5,128]{2,0,1:T(8,128)S(1)} fusion(bf16[512,5,1536]{2,0,1:T(8,128)(2,1)} %bitcast.279, bf16[5,1536,128]{2,1,0:T(8,128)(2,1)} %param.35), kind=kOutput, calls=%fused_computation.24 | convolution fusion | flops 1006632960 | bytes 11141120 | tf_op jit(solution)/shard_map/red,edf->ref/dot_general | solution.py:52
  312.5 12.2 %convert_bitcast_fusion = bf16[512,5,1536]{2,0,1:T(8,128)(2,1)} fusion(bf16[5,128,1536]{2,1,0:T(8,128)(2,1)S(1)} %copy-done, bf16[512,5,1536]{2,0,1:T(8,128)(2,1)} %bitcast.280, bf16[5,1536,128]{2,1,0:T(8,128)(2,1)} %param.36, f32[512,5,128]{2,0,1:T(8,128)S(1)} %convolution_bitcast_fusion.1), kind=kOutput, calls=%fused_computation.8 | convolution fusion | flops 2019164160 | bytes 20971520 | tf_op jit(solution)/shard_map/ref,efd->red/dot_general | solution.py:59
  324.7 1.7 fusion.60
  326.4 1.7 fusion.59
  328.0 1.7 fusion.58
  329.7 1.7 fusion.57
  331.4 1.7 fusion.56
  333.0 1.7 fusion.55
  334.7 1.7 fusion.54
  343.0 1.7 fusion.49
  344.6 1.7 fusion.48
  346.3 1.7 fusion.47
  349.6 1.7 fusion.45
  352.9 1.7 fusion.43
  354.6 1.7 fusion.42
  356.2 1.7 fusion.41
  359.6 1.7 fusion.39
  361.2 1.7 fusion.38
  362.9 1.7 fusion.37
  371.2 1.7 fusion.32
  372.8 1.7 fusion.31
  374.5 1.7 fusion.30
  377.8 5.1 %all-to-all-start.1 = ((bf16[32,16,5,1536]{3,1,2,0:T(8,128)(2,1)}), bf16[32,16,5,1536]{3,1,2,0:T(8,128)(2,1)}, u32[]{:S(2)}, u32[]{:S(2)}) async-start(bf16[32,16,5,1536]{3,1,2,0:T(8,128)(2,1)} %fusion.29), calls=%async_computation.2 | async-start | bytes 15728640 | tf_op jit(solution)/shard_map/all_to_all | solution.py:88
  383.8 91.3 %all-to-all-done.1 = bf16[32,16,5,1536]{3,1,2,0:T(8,128)(2,1)} async-done(((bf16[32,16,5,1536]{3,1,2,0:T(8,128)(2,1)}), bf16[32,16,5,1536]{3,1,2,0:T(8,128)(2,1)}, u32[]{:S(2)}, u32[]{:S(2)}) %all-to-all-start.1) | async-done | bytes 7864352 | tf_op jit(solution)/shard_map/all_to_all | solution.py:88
  475.1 4.9 bitcast_reduce_fusion
  480.0 2.8 copy.109
  482.8 4.3 reshape.388
  487.1 5.4 %gather_fusion.1 = bf16[512,1536]{1,0:T(8,128)(2,1)S(1)} fusion(bf16[640,1536]{1,0:T(8,128)(2,1)} %reshape.388, s32[1024]{0:T(1024)S(1)} %pad_clamp_fusion), kind=kCustom, calls=%fused_computation.1 | custom fusion | bytes 3147776 | tf_op jit(solution)/shard_map/jit(_take)/gather | solution.py:238
  492.5 2.8 multiply_reduce_fusion
  (116 shorter events, 51.7 us)
Async XLA Ops:
  7.2 305.3 %copy-start = (bf16[5,128,1536]{2,1,0:T(8,128)(2,1)S(1)}, bf16[5,128,1536]{2,1,0:T(8,128)(2,1)}, u32[]{:S(2)}) copy-start(bf16[5,128,1536]{2,1,0:T(8,128)(2,1)} %param.37) | copy-start | bytes 5898244
  7.2 40.2 %copy-start.13 = (s32[1,4]{1,0:T(1,128)S(1)}, s32[1,4]{1,0:T(1,128)}, u32[]{:S(2)}) copy-start(s32[1,4]{1,0:T(1,128)} %param.29) | copy-start | bytes 52
  7.2 40.7 %copy-start.12 = (f32[1536]{0:T(1024)S(1)}, f32[1536]{0:T(1024)}, u32[]{:S(2)}) copy-start(f32[1536]{0:T(1024)} %param.20) | copy-start | bytes 18436
  7.2 106.1 %all-reduce.2.cloned.1.call-start = ((), (), s32[]{:S(2)}) async-start(), calls=%async_computation.3 | async-start | bytes 917504 | tf_op jit(solution)/shard_map/psum | solution.py:132
  45.9 146.2 %reduce-scatter.2.cloned.1.call-start = ((), (), s32[]{:S(2)}) async-start(), calls=%async_computation.4 | async-start | bytes 983040 | tf_op jit(solution)/shard_map/reduce_scatter | solution.py:197
  53.9 0.6 copy-start.7
  53.9 0.6 copy-start.8
  128.7 9.0 %slice-start = ((bf16[4,57344]{1,0:T(4,128)(2,1)}), bf16[4,2048]{1,0:T(4,128)(2,1)S(1)}, s32[]{:S(2)}) async-start(bf16[4,57344]{1,0:T(4,128)(2,1)} %all-reduce.2.cloned.1.call-done), calls=%async_computation.5 | async-start | bytes 32768 | tf_op jit(solution)/shard_map/slice | solution.py:136
  128.9 9.0 %copy-start.3 = (bf16[256,1536]{1,0:T(8,128)(2,1)S(1)}, bf16[256,1536]{1,0:T(8,128)(2,1)}, u32[]{:S(2)}) copy-start(bf16[256,1536]{1,0:T(8,128)(2,1)} %param.19) | copy-start | bytes 2359300
  129.8 26.5 %copy-start.2 = (pred[256,2048]{0,1:T(8,128)(4,1)S(1)}, pred[256,2048]{0,1:T(8,128)(4,1)}, u32[]{:S(2)}) copy-start(pred[256,2048]{0,1:T(8,128)(4,1)} %fusion.6) | copy-start | bytes 1572868
  156.3 8.2 %copy-start.1 = (f32[2,2048,256,3]{2,1,3,0:T(8,128)S(1)}, f32[2,2048,256,3]{2,1,3,0:T(8,128)}, u32[]{:S(2)}) copy-start(f32[2,2048,256,3]{2,1,3,0:T(8,128)} %get-tuple-element.17) | copy-start | bytes 37748740
  156.3 8.3 %copy-start.6 = (bf16[2048,128]{0,1:T(8,128)(2,1)S(1)}, bf16[2048,128]{0,1:T(8,128)(2,1)}, u32[]{:S(2)}) copy-start(bf16[2048,128]{0,1:T(8,128)(2,1)} %copy.98) | copy-start | bytes 1572868
  164.6 3.6 copy-start.5
  164.6 5.1 %copy-start.9 = (s32[64,8]{0,1:T(8,128)S(1)}, s32[64,8]{0,1:T(8,128)}, u32[]{:S(2)}) copy-start(s32[64,8]{0,1:T(8,128)} %param.33) | copy-start | bytes 6148
  164.6 27.5 %copy-start.4 = (bf16[256,1536]{1,0:T(8,128)(2,1)S(1)}, bf16[256,1536]{1,0:T(8,128)(2,1)}, u32[]{:S(2)}) copy-start(bf16[256,1536]{1,0:T(8,128)(2,1)} %param.19) | copy-start | bytes 2359300
  164.6 28.6 %copy-start.10 = (f32[1536]{0:T(1024)S(1)}, f32[1536]{0:T(1024)}, u32[]{:S(2)}) copy-start(f32[1536]{0:T(1024)} %param.32) | copy-start | bytes 18436
  377.8 5.3 %copy-start.11 = (f32[64,8]{0,1:T(8,128)S(1)}, f32[64,8]{0,1:T(8,128)}, u32[]{:S(2)}) copy-start(f32[64,8]{0,1:T(8,128)} %param.34) | copy-start | bytes 6148
  377.8 97.3 %all-to-all-start.1 = ((bf16[32,16,5,1536]{3,1,2,0:T(8,128)(2,1)}), bf16[32,16,5,1536]{3,1,2,0:T(8,128)(2,1)}, u32[]{:S(2)}, u32[]{:S(2)}) async-start(bf16[32,16,5,1536]{3,1,2,0:T(8,128)(2,1)} %fusion.29), calls=%async_computation.2 | async-start | bytes 15728640 | tf_op jit(solution)/shard_map/all_to_all | solution.py:88
Sparse Core Ops, SparseCore 0:
  46.0 67.2 all-reduce.1
  169.8 22.1 reduce-scatter.1
